TPU v7x, 256 devices: a whole 4x4x8 slice. The times are simulated.
256 devices in a mesh: seq: 32 (over x, z), tensor: 8 (over y, core).
Axes of the slice: x: 4, y: 4, z: 8, core: 2. Of those that a mesh axis runs over, the one named last changes fastest.
Arguments:
- queries: bfloat16 [10240, 4096], P('seq', 'tensor'), may hold values from -8 to 8
- key_rows: bfloat16 [10240, 1024], P('seq', 'tensor'), may hold values from -8 to 8
- value_rows: bfloat16 [10240, 1024], P('seq', 'tensor'), may hold values from -6 to 6
- out_weight: bfloat16 [4096, 8192], P('tensor', 'seq'), may hold values from -0.09375 to 0.09375
- residual_in: bfloat16 [10240, 8192], P('seq'), may hold values from -0.1796875 to 0.1796875
- norm_gain: bfloat16 [8192], replicated, may hold values from 0.099609375 to 1.8984375
- prompt_lengths: int32 [18], replicated, may hold values from 1 to 5120, 10240 in all
Outputs:
- normed: bfloat16 [10240, 8192], P('seq')
- cache_keys: bfloat16 [22528, 1024], P('seq', 'tensor')
- cache_values: bfloat16 [22528, 1024], P('seq', 'tensor')
Inputs may be any that keep to these rules, and one draw needn't show every extreme that they name: `prompt_lengths`: the 18 lengths sum to 10240, and the largest is 5120.
All inputs are finite; a program needn't handle non-finite values.
Results may differ from a plain program's by a relative error of at most 0.019.
Values may be sent and summed in bfloat16 or wider, within the bound.
No kernel may reach another device: no remote copies, remote signals or barrier semaphores. Data moves between devices by JAX's collectives and lax.ppermute only.
A program may use at most 192 MiB of HBM per device.

v0:
```python
import math
import jax
import jax.numpy as jnp
from jax import lax
from jax.sharding import PartitionSpec as P

HD = 128
PAGE = 128
SLOT_DEV = 704


def position_of(stored, per_device, devices):
    half_block = per_device // 2
    device = stored // per_device
    offset = stored % per_device
    return jnp.where(
        offset < half_block,
        device * half_block + offset,
        (2 * devices - 1 - device) * half_block + offset - half_block,
    )


def stored_row(position, per_device, devices):
    half_block = per_device // 2
    block_index = position // half_block
    device = jnp.where(block_index < devices, block_index, 2 * devices - 1 - block_index)
    offset = position % half_block + jnp.where(block_index < devices, 0, half_block)
    return device * per_device + offset


def segment_of(position, lengths):
    doc_ends = jnp.cumsum(lengths, dtype=jnp.int32)
    return jnp.sum(
        (position[:, None] >= doc_ends[None, :]).astype(jnp.int32), axis=1, dtype=jnp.int32
    )


def slot_source(slot_ids, lengths, page_size):
    padded = (lengths + page_size - 1) // page_size * page_size
    page_ends = jnp.cumsum(padded, dtype=jnp.int32)
    page_starts = page_ends - padded
    doc_ends = jnp.cumsum(lengths, dtype=jnp.int32)
    doc_starts = doc_ends - lengths
    prompt = jnp.sum(
        (slot_ids[:, None] >= page_ends[None, :]).astype(jnp.int32), axis=1, dtype=jnp.int32
    )
    clipped = jnp.minimum(prompt, lengths.shape[0] - 1)
    within = slot_ids - jnp.take(page_starts, clipped)
    is_live = (prompt < lengths.shape[0]) & (within < jnp.take(lengths, clipped))
    return (jnp.take(doc_starts, clipped) + within, is_live)


def body(queries, key_rows, value_rows, out_weight, residual_in, norm_gain, prompt_lengths):
    seq_count = lax.axis_size("seq")
    seq_index = lax.axis_index("seq")
    per_device = queries.shape[0]
    kv_local = key_rows.shape[1] // HD
    group_size = queries.shape[1] // (kv_local * HD)
    score_scale = 1.0 / math.sqrt(HD)
    local_rows = jnp.arange(per_device, dtype=jnp.int32) + seq_index * per_device
    my_position = position_of(local_rows, per_device, seq_count)
    my_segment = segment_of(my_position, prompt_lengths)
    grouped = queries.reshape(per_device, kv_local, group_size, HD)
    key_piece = lax.all_gather(key_rows, "seq", axis=0, tiled=True)
    value_piece = lax.all_gather(value_rows, "seq", axis=0, tiled=True)
    piece_rows = key_piece.shape[0]
    key_position = position_of(jnp.arange(piece_rows, dtype=jnp.int32), per_device, seq_count)
    key_segment = segment_of(key_position, prompt_lengths)
    allowed = (key_position[None, :] <= my_position[:, None]) & (
        key_segment[None, :] == my_segment[:, None]
    )
    top_old = jnp.full((kv_local, group_size, per_device), -1e30, jnp.float32)
    scores = (
        jnp.einsum(
            "qgjd,kgd->gjqk",
            grouped,
            key_piece.reshape(piece_rows, kv_local, HD),
            preferred_element_type=jnp.float32,
        )
        * score_scale
    )
    scores = jnp.where(allowed, scores, -1e30)
    top_new = jnp.maximum(top_old, jnp.max(scores, axis=-1))
    weights = jnp.where(allowed, jnp.exp(scores - top_new[..., None]), 0.0)
    total_new = jnp.sum(weights, axis=-1)
    accum_new = jnp.einsum(
        "gjqk,kgd->gjqd",
        weights.astype(jnp.bfloat16),
        value_piece.reshape(piece_rows, kv_local, HD),
        preferred_element_type=jnp.float32,
    )
    attended = jnp.transpose(accum_new / total_new[..., None], (2, 0, 1, 3))
    attended = attended.reshape(per_device, -1).astype(jnp.bfloat16)
    partial_value = jnp.dot(
        attended,
        lax.all_gather(out_weight, "seq", axis=1, tiled=True),
        preferred_element_type=jnp.float32,
    )
    projected = lax.psum(partial_value.astype(jnp.bfloat16), "tensor").astype(jnp.float32)
    hidden = residual_in.astype(jnp.float32) + projected
    mean_square = jnp.mean(hidden * hidden, axis=-1, keepdims=True)
    normed = (hidden * lax.rsqrt(mean_square + 1e-05) * norm_gain.astype(jnp.float32)).astype(
        jnp.bfloat16
    )
    slot_ids = seq_index * SLOT_DEV + jnp.arange(SLOT_DEV, dtype=jnp.int32)
    source, is_live = slot_source(slot_ids, prompt_lengths, PAGE)
    target = stored_row(source, per_device, seq_count)
    empty_cache = jnp.zeros((SLOT_DEV, kv_local * HD), jnp.bfloat16)
    key_piece = lax.all_gather(key_rows, "seq", axis=0, tiled=True)
    value_piece = lax.all_gather(value_rows, "seq", axis=0, tiled=True)
    piece_rows = key_piece.shape[0]
    found = is_live & (target >= 0) & (target < piece_rows)
    safe_index = jnp.clip(target, 0, piece_rows - 1)
    cache_keys = jnp.where(found[:, None], jnp.take(key_piece, safe_index, axis=0), empty_cache)
    cache_values = jnp.where(found[:, None], jnp.take(value_piece, safe_index, axis=0), empty_cache)
    return (normed, cache_keys, cache_values)


def solution(mesh):
    return jax.shard_map(
        body,
        mesh=mesh,
        in_specs=(
            P("seq", "tensor"),
            P("seq", "tensor"),
            P("seq", "tensor"),
            P("tensor", "seq"),
            P("seq", None),
            P(),
            P(),
        ),
        out_specs=(P("seq", None), P("seq", "tensor"), P("seq", "tensor")),
        check_vma=False,
    )
```

profile of v0, /device:TPU:1, one launch (start us, length us, event | category | flops | bytes accessed | tf_op | source)
XLA Modules:
  0.0 381.7 jit_solution(8324192015222926720)
XLA Ops:
  7.2 0.7 all-gather.4.cloned.1.call-update
  8.0 0.7 all-gather.6.cloned.1.call-update
  8.7 0.7 all-gather.8.cloned.1.call-update
  9.4 0.7 copy.17
  10.5 0.2 convert_reduce_fusion
  10.8 4.6 %compare_and_fusion = pred[320,10240]{1,0:T(8,128)(4,1)} fusion(s32[10240]{0:T(1024)S(1)} %convert_reduce_fusion, s32[10240]{0:T(1024)S(1)} %fusion.38, s32[320]{0:T(512)S(1)} %convert_reduce_fusion.2, s32[320]{0:T(512)S(1)} %add_select_fusion.5), kind=kLoop, calls=%fused_computation.10 | loop fusion | flops 9830400 | bytes 3361280 | tf_op jit(solution)/shard_map/and | solution.py:69
  15.3 74.5 %all-gather.4.cloned.1.call-done = bf16[10240,128]{1,0:T(8,128)(2,1)} async-done(((bf16[320,128]{1,0:T(8,128)(2,1)}), bf16[10240,128]{1,0:T(8,128)(2,1)}) %all-gather.4.cloned.1.call-update) | async-done | bytes 2621456 | tf_op jit(solution)/shard_map/all_gather | solution.py:64
  89.8 22.6 %fusion = (f32[4,320]{1,0:T(4,128)S(1)}, f32[10240,320,4]{0,1,2:T(8,128)}) fusion(pred[320,10240]{1,0:T(8,128)(4,1)} %compare_and_fusion, bf16[10240,128]{1,0:T(8,128)(2,1)} %all-gather.4.cloned.1.call-done, bf16[320,512]{1,0:T(8,128)(2,1)S(1)} %copy-done), kind=kOutput, calls=%fused_computation.4 | convolution fusion | flops 3394763520 | bytes 58659840 | tf_op jit(solution)/shard_map/qgjd,kgd->gjqk/dot_general | solution.py:74
  112.4 22.7 %fusion.1 = f32[4,320]{1,0:T(4,128)S(1)} fusion(f32[10240,320,4]{0,1,2:T(8,128)} %get-tuple-element.66, f32[4,320]{1,0:T(4,128)S(1)} %broadcast_maximum_fusion, pred[320,10240]{1,0:T(8,128)(4,1)} %compare_and_fusion), kind=kLoop, calls=%fused_computation.5 | loop fusion | flops 65534720 | bytes 55715840 | tf_op jit(solution)/shard_map/reduce_sum | solution.py:85
  135.1 33.1 %all-gather.6.cloned.1.call-done = bf16[10240,128]{1,0:T(8,128)(2,1)} async-done(((bf16[320,128]{1,0:T(8,128)(2,1)}), bf16[10240,128]{1,0:T(8,128)(2,1)}) %all-gather.6.cloned.1.call-update) | async-done | bytes 2621456 | tf_op jit(solution)/shard_map/all_gather | solution.py:65
  168.2 23.3 %fusion.20 = bf16[320,1,4,128]{3,0,2,1:T(8,128)(2,1)S(1)} fusion(bf16[10240,128]{1,0:T(8,128)(2,1)} %all-gather.6.cloned.1.call-done, f32[10240,320,4]{0,1,2:T(8,128)} %get-tuple-element.66, f32[4,320]{1,0:T(4,128)S(1)} %broadcast_maximum_fusion, pred[320,10240]{1,0:T(8,128)(4,1)} %compare_and_fusion, f32[4,320]{1,0:T(4,128)S(1)} %fusion.1), kind=kOutput, calls=%fused_computation.20 | convolution fusion | flops 3421306880 | bytes 58664960 | tf_op jit(solution)/shard_map/gjqk,kgd->gjqd/dot_general | solution.py:86
  191.6 0.3 copy.19
  191.9 80.5 %all-gather.8.cloned.1.call-done = bf16[512,8192]{1,0:T(8,128)(2,1)} async-done(((bf16[512,256]{1,0:T(8,128)(2,1)}), bf16[512,8192]{1,0:T(8,128)(2,1)}) %all-gather.8.cloned.1.call-update) | async-done | bytes 8388624 | tf_op jit(solution)/shard_map/all_gather | solution.py:96
  272.4 8.1 %convolution_convert_fusion = bf16[320,8192]{1,0:T(8,128)(2,1)} fusion(bf16[512,8192]{1,0:T(8,128)(2,1)} %all-gather.8.cloned.1.call-done, bf16[40,8,4,128]{3,2,1,0:T(4,128)(2,1)S(1)} %bitcast.120), kind=kOutput, calls=%fused_computation.11 | convolution fusion | flops 2686976000 | bytes 13959168 | tf_op jit(solution)/shard_map/dot_general | solution.py:94
  280.9 0.7 fusion.58
  281.6 0.7 fusion.57
  282.3 0.7 fusion.55
  283.1 33.8 %compare_and_fusion.3 = (pred[704]{0:T(1024)(128)(4,1)S(1)}, s32[704]{0:T(1024)S(1)}) fusion(s32[704]{0:T(1024)S(1)} %convert_reduce_fusion.1, s32[]{:T(128)} %bitcast.44, s32[]{:T(128)} %bitcast.43, s32[]{:T(128)} %bitcast.42, s32[]{:T(128)} %bitcast.41, s32[]{:T(128)} %bitcast.40, s32[]{:T(128)} %bitcast.39, s32[]{:T(128)} %bitcast.38, s32[]{:T(128)} %bitcast.37, ...), kind=kLoop, calls=%fused_computation.64 | loop fusion | flops 75328 | bytes 6556 | tf_op jit(solution)/shard_map/and | solution.py:112
  317.0 2.0 gather_fusion
  319.0 3.9 %gather_fusion.1 = bf16[704,128]{1,0:T(8,128)(2,1)S(1)} fusion(bf16[10240,128]{1,0:T(8,128)(2,1)} %all-gather.6.cloned.1.call-done, s32[1024]{0:T(1024)S(1)} %pad_clamp_fusion), kind=kCustom, calls=%fused_computation.1.clone | custom fusion | bytes 363264 | tf_op jit(solution)/shard_map/jit(_take)/gather | solution.py:115
  322.9 1.0 select_select_fusion
  323.9 38.1 %all-reduce.2.cloned.1.call-done = bf16[320,8192]{1,0:T(8,128)(2,1)} async-done(((bf16[320,8192]{1,0:T(8,128)(2,1)}), bf16[320,8192]{1,0:T(8,128)(2,1)}) %all-reduce.2.cloned.1.call-update) | async-done | bytes 5242896 | tf_op jit(solution)/shard_map/psum | solution.py:99
  362.0 6.0 %multiply_reduce_fusion = f32[320]{0:T(512)S(1)} fusion(bf16[320,8192]{1,0:T(8,128)(2,1)} %all-reduce.2.cloned.1.call-done, bf16[320,8192]{1,0:T(8,128)(2,1)} %param.15), kind=kLoop, calls=%fused_computation.13 | loop fusion | flops 13106880 | bytes 10487040 | tf_op jit(solution)/shard_map/reduce_sum | solution.py:101
  368.0 7.1 %multiply_convert_fusion = bf16[320,8192]{1,0:T(8,128)(2,1)} fusion(bf16[320,8192]{1,0:T(8,128)(2,1)S(1)} %copy-done.2, bf16[320,8192]{1,0:T(8,128)(2,1)} %param.15, f32[8192]{0:T(1024)S(1)} %convert_element_type.49, f32[320]{0:T(512)S(1)} %add_rsqrt_fusion), kind=kLoop, calls=%fused_computation.12 | loop fusion | flops 15728640 | bytes 15762688 | tf_op jit(solution)/shard_map/convert_element_type | solution.py:102
  (35 shorter events, 0.9 us)
Async XLA Ops:
  7.2 82.6 %copy-start = (bf16[320,512]{1,0:T(8,128)(2,1)S(1)}, bf16[320,512]{1,0:T(8,128)(2,1)}, u32[]{:S(2)}) copy-start(bf16[320,512]{1,0:T(8,128)(2,1)} %param.11) | copy-start | bytes 983044
  7.2 82.6 %all-gather.4.cloned.1.call-start = ((), (), s32[]{:S(2)}) async-start(), calls=%async_computation | async-start | bytes 2703360 | tf_op jit(solution)/shard_map/all_gather | solution.py:64
  7.9 160.3 %all-gather.6.cloned.1.call-start = ((), (), s32[]{:S(2)}) async-start(), calls=%async_computation.1 | async-start | bytes 2703360 | tf_op jit(solution)/shard_map/all_gather | solution.py:65
  8.7 263.7 %all-gather.8.cloned.1.call-start = ((), (), s32[]{:S(2)}) async-start(), calls=%async_computation.2 | async-start | bytes 8650752 | tf_op jit(solution)/shard_map/all_gather | solution.py:96
  9.4 352.6 %all-reduce.2.cloned.1.call-start = ((), (), s32[]{:S(2)}) async-start(), calls=%async_computation.3 | async-start | bytes 10485760 | tf_op jit(solution)/shard_map/psum | solution.py:99
  191.9 88.7 %copy-start.4 = (s32[18]{0:T(128)S(1)}, s32[18]{0:T(128)}, u32[]{:S(2)}) copy-start(s32[18]{0:T(128)} %param.17) | copy-start | bytes 220
  191.9 89.0 %copy-start.5 = (bf16[8192]{0:T(1024)(128)(2,1)S(1)}, bf16[8192]{0:T(1024)(128)(2,1)}, u32[]{:S(2)}) copy-start(bf16[8192]{0:T(1024)(128)(2,1)} %param.16) | copy-start | bytes 49156
  272.4 44.6 %copy-start.3 = (bf16[10240,128]{1,0:T(8,128)(2,1)S(1)}, bf16[10240,128]{1,0:T(8,128)(2,1)}, u32[]{:S(2)}) copy-start(bf16[10240,128]{1,0:T(8,128)(2,1)} %all-gather.4.cloned.1.call-done) | copy-start | bytes 7864324
  362.0 6.0 %copy-start.2 = (bf16[320,8192]{1,0:T(8,128)(2,1)S(1)}, bf16[320,8192]{1,0:T(8,128)(2,1)}, u32[]{:S(2)}) copy-start(bf16[320,8192]{1,0:T(8,128)(2,1)} %all-reduce.2.cloned.1.call-done) | copy-start | bytes 15728644
  362.0 13.1 %copy-start.1 = (bf16[320,512]{1,0:T(8,128)(2,1)S(1)}, bf16[320,512]{1,0:T(8,128)(2,1)}, u32[]{:S(2)}) copy-start(bf16[320,512]{1,0:T(8,128)(2,1)} %param.11) | copy-start | bytes 983044
Sparse Core Ops, SparseCore 0:
  10.6 79.1 all-gather.3
  92.4 75.8 all-gather.5
  170.7 101.6 all-gather.7
  280.7 81.3 all-reduce.1
where the time goes:
time: 382 us
  waiting for transfers between devices  228 us (60%)
  other arithmetic  76 us (20%)
  matrix products  54.1 us (14%)
  between operations  13.9 us (4%)
  local copies, waits for them, and re-layouts  9.24 us (2%)
    all_gather x1, waiting for transfers between devices, body(): lax.all_gather(out_weight, 'seq', axis=1, tiled=True)  80.5 us
    all_gather x1, waiting for transfers between devices, body(): key_piece = lax.all_gather(key_rows, 'seq', axis=0, tiled=True)  74.5 us
    psum x1, waiting for transfers between devices, body(): lax.psum(partial_value.astype(jnp.bfloat16), 'tensor').astype(jnp.float32)  38.1 us
    and x1, other arithmetic, body(): found = is_live & (target >= 0) & (target < piece_rows)  33.8 us
    all_gather x1, waiting for transfers between devices, body(): value_piece = lax.all_gather(value_rows, 'seq', axis=0, tiled=True)  33.1 us
    dot_general x1, matrix products, body(): jnp.einsum('gjqk,kgd->gjqd', weights.astype(jnp.bfloat16), value_piece.re...  23.3 us
    reduce_sum x1, other arithmetic, body(): total_new = jnp.sum(weights, axis=-1)  22.7 us
    dot_general x1, matrix products, body(): jnp.einsum('qgjd,kgd->gjqk', grouped, key_piece.reshape(piece_rows, kv_lo...  22.6 us
  transfers between devices with their start and end apart: 4, of which 4 were waited for; matrix products, arithmetic and copies ran while one was open for 31% of the time, Pallas kernels for 0%

commit v1 on v0

--- a/solution.py
+++ b/solution.py
@@ -96,7 +96,9 @@
         lax.all_gather(out_weight, "seq", axis=1, tiled=True),
         preferred_element_type=jnp.float32,
     )
-    projected = lax.psum(partial_value.astype(jnp.bfloat16), "tensor").astype(jnp.float32)
+    projected = jnp.sum(
+        lax.all_gather(partial_value.astype(jnp.bfloat16), "tensor"), axis=0
+    ).astype(jnp.float32)
     hidden = residual_in.astype(jnp.float32) + projected
     mean_square = jnp.mean(hidden * hidden, axis=-1, keepdims=True)
     normed = (hidden * lax.rsqrt(mean_square + 1e-05) * norm_gain.astype(jnp.float32)).astype(

time: 382 us -> 514 us (1.35)
  waiting for transfers between devices: 228 us -> 342 us
  other arithmetic: 76 us -> 93.3 us
    all_gather x0 -> x1, waiting for transfers between devices: none -> 152 us  [body(): lax.all_gather(partial_value.astype(jnp.bfloat16), 'tensor')]
    psum x1 -> x0, waiting for transfers between devices: 38.1 us -> none  [body(): lax.psum(partial_value.astype(jnp.bfloat16), 'tensor').astype(jnp.float32)]
    reduce_sum x0 -> x1, other arithmetic: none -> 17.1 us  [body(): jnp.sum(lax.all_gather(partial_value.astype(jnp.bfloat16), 'tensor'), axi...]
  transfers between devices with their start and end apart: 4 -> 4, of which waited for: 4 -> 4; matrix products, arithmetic and copies ran while one was open for 31% -> 23% of each run, Pallas kernels for 0% -> 0%
where the time goes in v1:
time: 514 us; the launch traced here: 513 us
  waiting for transfers between devices  342 us (67%)
  other arithmetic  93.3 us (18%)
  matrix products  54.1 us (11%)
  between operations  13.9 us (3%)
  local copies, waits for them, and re-layouts  9.3 us (2%)
    all_gather x1, waiting for transfers between devices, body(): lax.all_gather(partial_value.astype(jnp.bfloat16), 'tensor')  152 us
    all_gather x1, waiting for transfers between devices, body(): lax.all_gather(out_weight, 'seq', axis=1, tiled=True)  80.5 us
    all_gather x1, waiting for transfers between devices, body(): key_piece = lax.all_gather(key_rows, 'seq', axis=0, tiled=True)  74.5 us
    and x1, other arithmetic, body(): found = is_live & (target >= 0) & (target < piece_rows)  34 us
    all_gather x1, waiting for transfers between devices, body(): value_piece = lax.all_gather(value_rows, 'seq', axis=0, tiled=True)  33.1 us
    dot_general x1, matrix products, body(): jnp.einsum('gjqk,kgd->gjqd', weights.astype(jnp.bfloat16), value_piece.re...  23.3 us
    reduce_sum x1, other arithmetic, body(): total_new = jnp.sum(weights, axis=-1)  22.7 us
    dot_general x1, matrix products, body(): jnp.einsum('qgjd,kgd->gjqk', grouped, key_piece.reshape(piece_rows, kv_lo...  22.6 us
  transfers between devices with their start and end apart: 4, of which 4 were waited for; matrix products, arithmetic and copies ran while one was open for 23% of the time, Pallas kernels for 0%

profile of v1, /device:TPU:1, one launch (start us, length us, event | category | flops | bytes accessed | tf_op | source)
XLA Modules:
  0.0 513.0 jit_solution(1100827314483082953)
XLA Ops:
  7.2 0.7 all-gather.6.cloned.1.call-update
  8.0 0.7 all-gather.8.cloned.1.call-update
  8.7 0.7 all-gather.10.cloned.1.call-update
  9.4 0.7 copy.17
  10.8 4.6 compare_and_fusion
  15.3 74.5 %all-gather.6.cloned.1.call-done = bf16[10240,128]{1,0:T(8,128)(2,1)} async-done(((bf16[320,128]{1,0:T(8,128)(2,1)}), bf16[10240,128]{1,0:T(8,128)(2,1)}) %all-gather.6.cloned.1.call-update) | async-done | bytes 2621456 | tf_op jit(solution)/shard_map/all_gather | solution.py:64
  89.8 22.6 %fusion = (f32[4,320]{1,0:T(4,128)S(1)}, f32[10240,320,4]{0,1,2:T(8,128)}) fusion(pred[320,10240]{1,0:T(8,128)(4,1)} %compare_and_fusion, bf16[10240,128]{1,0:T(8,128)(2,1)} %all-gather.6.cloned.1.call-done, bf16[320,512]{1,0:T(8,128)(2,1)S(1)} %copy-done), kind=kOutput, calls=%fused_computation.4 | convolution fusion | flops 3394763520 | bytes 58659840 | tf_op jit(solution)/shard_map/qgjd,kgd->gjqk/dot_general | solution.py:74
  112.4 22.7 %fusion.1 = f32[4,320]{1,0:T(4,128)S(1)} fusion(f32[10240,320,4]{0,1,2:T(8,128)} %get-tuple-element.66, f32[4,320]{1,0:T(4,128)S(1)} %broadcast_maximum_fusion, pred[320,10240]{1,0:T(8,128)(4,1)} %compare_and_fusion), kind=kLoop, calls=%fused_computation.5 | loop fusion | flops 65534720 | bytes 55715840 | tf_op jit(solution)/shard_map/reduce_sum | solution.py:85
  135.1 33.1 %all-gather.8.cloned.1.call-done = bf16[10240,128]{1,0:T(8,128)(2,1)} async-done(((bf16[320,128]{1,0:T(8,128)(2,1)}), bf16[10240,128]{1,0:T(8,128)(2,1)}) %all-gather.8.cloned.1.call-update) | async-done | bytes 2621456 | tf_op jit(solution)/shard_map/all_gather | solution.py:65
  168.2 23.3 %fusion.20 = bf16[320,1,4,128]{3,0,2,1:T(8,128)(2,1)S(1)} fusion(bf16[10240,128]{1,0:T(8,128)(2,1)} %all-gather.8.cloned.1.call-done, f32[10240,320,4]{0,1,2:T(8,128)} %get-tuple-element.66, f32[4,320]{1,0:T(4,128)S(1)} %broadcast_maximum_fusion, pred[320,10240]{1,0:T(8,128)(4,1)} %compare_and_fusion, f32[4,320]{1,0:T(4,128)S(1)} %fusion.1), kind=kOutput, calls=%fused_computation.20 | convolution fusion | flops 3421306880 | bytes 58664960 | tf_op jit(solution)/shard_map/gjqk,kgd->gjqd/dot_general | solution.py:86
  191.6 0.3 copy.19
  191.9 80.5 %all-gather.10.cloned.1.call-done = bf16[512,8192]{1,0:T(8,128)(2,1)} async-done(((bf16[512,256]{1,0:T(8,128)(2,1)}), bf16[512,8192]{1,0:T(8,128)(2,1)}) %all-gather.10.cloned.1.call-update) | async-done | bytes 8388624 | tf_op jit(solution)/shard_map/all_gather | solution.py:96
  272.4 8.1 %convolution_convert_fusion = bf16[320,8192]{1,0:T(8,128)(2,1)} fusion(bf16[512,8192]{1,0:T(8,128)(2,1)} %all-gather.10.cloned.1.call-done, bf16[40,8,4,128]{3,2,1,0:T(4,128)(2,1)S(1)} %bitcast.122), kind=kOutput, calls=%fused_computation.11 | convolution fusion | flops 2686976000 | bytes 13959168 | tf_op jit(solution)/shard_map/dot_general | solution.py:94
  280.9 0.7 fusion.58
  281.6 0.7 fusion.57
  282.3 0.7 fusion.55
  283.1 34.0 %compare_and_fusion.3 = (pred[704]{0:T(1024)(128)(4,1)S(1)}, s32[704]{0:T(1024)S(1)}) fusion(s32[704]{0:T(1024)S(1)} %convert_reduce_fusion.1, s32[]{:T(128)} %bitcast.45, s32[]{:T(128)} %bitcast.44, s32[]{:T(128)} %bitcast.43, s32[]{:T(128)} %bitcast.42, s32[]{:T(128)} %bitcast.41, s32[]{:T(128)} %bitcast.40, s32[]{:T(128)} %bitcast.39, s32[]{:T(128)} %bitcast.38, ...), kind=kLoop, calls=%fused_computation.64 | loop fusion | flops 75328 | bytes 6556 | tf_op jit(solution)/shard_map/and | solution.py:114
  317.1 2.0 gather_fusion
  319.2 4.0 gather_fusion.1
  323.2 1.0 select_select_fusion
  324.2 152.1 %all-gather.12.cloned.1.call-done = bf16[2560,8192]{1,0:T(8,128)(2,1)} async-done(((bf16[320,8192]{1,0:T(8,128)(2,1)}), bf16[2560,8192]{1,0:T(8,128)(2,1)}) %all-gather.12.cloned.1.call-update) | async-done | bytes 41943056 | tf_op jit(solution)/shard_map/all_gather | solution.py:100
  476.3 17.1 %reduce_sum.60 = bf16[320,8192]{1,0:T(8,128)(2,1)} reduce(bf16[8,320,8192]{2,1,0:T(8,128)(2,1)} %bitcast.121, bf16[]{:T(256)} %constant.127.clone.1), dimensions={0}, to_apply=%region_5.6 | reduce | flops 18350080 | bytes 47185920 | tf_op jit(solution)/shard_map/reduce_sum | solution.py:99
  493.4 6.0 %multiply_reduce_fusion = f32[320]{0:T(512)S(1)} fusion(bf16[320,8192]{1,0:T(8,128)(2,1)} %reduce_sum.60, bf16[320,8192]{1,0:T(8,128)(2,1)} %param.15), kind=kLoop, calls=%fused_computation.13 | loop fusion | flops 13106880 | bytes 10487040 | tf_op jit(solution)/shard_map/reduce_sum | solution.py:103
  499.4 7.1 %multiply_convert_fusion = bf16[320,8192]{1,0:T(8,128)(2,1)} fusion(bf16[320,8192]{1,0:T(8,128)(2,1)S(1)} %copy-done.2, bf16[320,8192]{1,0:T(8,128)(2,1)} %param.15, f32[8192]{0:T(1024)S(1)} %convert_element_type.51, f32[320]{0:T(512)S(1)} %add_rsqrt_fusion), kind=kLoop, calls=%fused_computation.12 | loop fusion | flops 15728640 | bytes 15762688 | tf_op jit(solution)/shard_map/convert_element_type | solution.py:104
  (36 shorter events, 1.2 us)
Async XLA Ops:
  7.2 82.6 %copy-start = (bf16[320,512]{1,0:T(8,128)(2,1)S(1)}, bf16[320,512]{1,0:T(8,128)(2,1)}, u32[]{:S(2)}) copy-start(bf16[320,512]{1,0:T(8,128)(2,1)} %param.11) | copy-start | bytes 983044
  7.2 82.6 %all-gather.6.cloned.1.call-start = ((), (), s32[]{:S(2)}) async-start(), calls=%async_computation | async-start | bytes 2703360 | tf_op jit(solution)/shard_map/all_gather | solution.py:64
  7.9 160.3 %all-gather.8.cloned.1.call-start = ((), (), s32[]{:S(2)}) async-start(), calls=%async_computation.1 | async-start | bytes 2703360 | tf_op jit(solution)/shard_map/all_gather | solution.py:65
  8.7 263.7 %all-gather.10.cloned.1.call-start = ((), (), s32[]{:S(2)}) async-start(), calls=%async_computation.2 | async-start | bytes 8650752 | tf_op jit(solution)/shard_map/all_gather | solution.py:96
  9.4 466.9 %all-gather.12.cloned.1.call-start = ((), (), s32[]{:S(2)}) async-start(), calls=%async_computation.3 | async-start | bytes 47185920 | tf_op jit(solution)/shard_map/all_gather | solution.py:100
  191.9 88.7 %copy-start.4 = (s32[18]{0:T(128)S(1)}, s32[18]{0:T(128)}, u32[]{:S(2)}) copy-start(s32[18]{0:T(128)} %param.17) | copy-start | bytes 220
  191.9 89.0 %copy-start.5 = (bf16[8192]{0:T(1024)(128)(2,1)S(1)}, bf16[8192]{0:T(1024)(128)(2,1)}, u32[]{:S(2)}) copy-start(bf16[8192]{0:T(1024)(128)(2,1)} %param.16) | copy-start | bytes 49156
  272.4 44.7 %copy-start.3 = (bf16[10240,128]{1,0:T(8,128)(2,1)S(1)}, bf16[10240,128]{1,0:T(8,128)(2,1)}, u32[]{:S(2)}) copy-start(bf16[10240,128]{1,0:T(8,128)(2,1)} %all-gather.6.cloned.1.call-done) | copy-start | bytes 7864324
  493.4 6.0 %copy-start.2 = (bf16[320,8192]{1,0:T(8,128)(2,1)S(1)}, bf16[320,8192]{1,0:T(8,128)(2,1)}, u32[]{:S(2)}) copy-start(bf16[320,8192]{1,0:T(8,128)(2,1)} %reduce_sum.60) | copy-start | bytes 15728644
  493.4 13.1 %copy-start.1 = (bf16[320,512]{1,0:T(8,128)(2,1)S(1)}, bf16[320,512]{1,0:T(8,128)(2,1)}, u32[]{:S(2)}) copy-start(bf16[320,512]{1,0:T(8,128)(2,1)} %param.11) | copy-start | bytes 983044
Sparse Core Ops, SparseCore 0:
  10.6 79.1 all-gather.5
  92.4 75.8 all-gather.7
  170.7 101.6 all-gather.9
  280.7 195.5 all-gather.11
